TPU v7x, 32 devices: a whole 2x2x4 slice. The times are simulated.
32 devices in a mesh: pair: 4 (over z), src: 2 (over x), tgt: 4 (over y, core).
Axes of the slice: x: 2, y: 2, z: 4, core: 2. Of those that a mesh axis runs over, the one named last changes fastest.
Arguments:
- src_cells: float32 [4, 30, 4096], P('pair', None, 'src'), may hold values from -17 to 17
- final_cells: float32 [30, 4096], P(None, 'tgt'), may hold values from -17 to 17
- growth: float32 [4, 4096], P('pair', 'src'), may hold values from 0.5 to 2
- live: int32 [5], replicated, may hold values from 1024 to 4096, as said below
- final_fates: float32 [40, 4096], P(None, 'tgt'), may hold values from 0 to 1
Outputs:
- fate_maps: float32 [4, 40, 4096], P('pair', None, ('src', 'tgt'))
- potentials: float32 [4, 4096], P('pair', 'src')
Inputs may be any that keep to these rules, and one draw needn't show every extreme that they name: `live`: every count is at least 1024 and one snapshot fills all 4096 slots.
All inputs are finite; a program needn't handle non-finite values.
Results may differ from a plain program's by a relative error of at most 0.0049.
Values may be sent and summed in bfloat16 or wider, within the bound.
No kernel may reach another device: no remote copies, remote signals or barrier semaphores. Data moves between devices by JAX's collectives and lax.ppermute only.
A program may use at most 64 MiB of HBM per device.

v0:
```python
import jax
import jax.numpy as jnp
from jax import lax
from jax.sharding import PartitionSpec as P

ITERS = 8
EPS = 0.1
LAM = 1.0
NEG = -1e30


def joined(shard, axis, combine):
    everything = jax.tree.map(lambda part: lax.all_gather(part, axis), shard)
    leading = jax.tree.map(lambda part: part[0], everything)

    def step(k, so_far):
        return combine(so_far, jax.tree.map(lambda part: part[k], everything))

    return lax.fori_loop(1, lax.axis_size(axis), step, leading)


def shifted(shard, axis, by):
    devices = lax.axis_size(axis)
    pairs = [(i, i + by) for i in range(devices) if 0 <= i + by < devices]
    return lax.ppermute(shard, axis, pairs)


def from_root(shard, axis, root):
    mine = lax.axis_index(axis) == root
    return lax.psum(jnp.where(mine, shard, jnp.zeros_like(shard)), axis)


def combine(first, second):
    peak = jnp.maximum(first[0], second[0])
    return (peak, first[1] * jnp.exp(first[0] - peak) + second[1] * jnp.exp(second[0] - peak))


def column_lse(col_scores):
    peak = jnp.max(col_scores, axis=0)
    totals = jnp.sum(jnp.exp(col_scores - peak[None, :]), axis=0)
    return joined((peak, totals), "src", combine)


def row_lse(row_scores):
    peak = jnp.max(row_scores, axis=1)
    totals = jnp.sum(jnp.exp(row_scores - peak[:, None]), axis=1)
    return joined((peak, totals), "tgt", combine)


def local(src_cells, final_cells, growth, live, final_fates):
    pair_count = lax.axis_size("pair")
    src_count = lax.axis_size("src")
    tgt_count = lax.axis_size("tgt")
    pair_rank = lax.axis_index("pair")
    src_rank = lax.axis_index("src")
    tgt_rank = lax.axis_index("tgt")
    shrink = LAM / (LAM + EPS)
    source_pos = src_cells[0]
    src_width = source_pos.shape[1]
    tgt_width = final_cells.shape[1]
    share_width = src_width // tgt_count
    tgt_ratio = tgt_count // src_count
    owner_rank = tgt_rank // tgt_ratio
    offset_in = tgt_rank % tgt_ratio * tgt_width
    is_last = pair_rank == pair_count - 1
    arrived = shifted(source_pos, "pair", -1)
    owner_cells = from_root(arrived, "src", owner_rank)
    target_pos = jnp.where(
        is_last, final_cells, lax.dynamic_slice_in_dim(owner_cells, offset_in, tgt_width, 1)
    )
    cross = lax.dot_general(
        source_pos,
        target_pos,
        (((0,), (0,)), ((), ())),
        precision=lax.Precision.HIGHEST,
        preferred_element_type=jnp.float32,
    )
    src_sq = jnp.sum(source_pos * source_pos, axis=0)
    tgt_sq = jnp.sum(target_pos * target_pos, axis=0)
    cost_tile = (src_sq[:, None] + tgt_sq[None, :] - 2.0 * cross) / (2.0 * source_pos.shape[0])
    live_now = lax.dynamic_index_in_dim(live, pair_rank, keepdims=False)
    live_next = lax.dynamic_index_in_dim(live, pair_rank + 1, keepdims=False)
    src_index = src_rank * src_width + jnp.arange(src_width, dtype=jnp.int32)
    tgt_index = tgt_rank * tgt_width + jnp.arange(tgt_width, dtype=jnp.int32)
    share_index = (src_rank * tgt_count + tgt_rank) * share_width + jnp.arange(
        share_width, dtype=jnp.int32
    )
    live_src = src_index < live_now
    live_tgt = tgt_index < live_next
    live_share = share_index < live_now
    log_mass_a = jnp.where(
        live_src, jnp.log(growth[0]) - jnp.log(live_now.astype(jnp.float32)), NEG
    )
    log_mass_b = jnp.where(
        live_tgt, -jnp.log(live_next.astype(jnp.float32)) * jnp.ones((tgt_width,), jnp.float32), NEG
    )
    pot_src = jnp.zeros((src_width,), jnp.float32)
    pot_tgt = jnp.zeros((tgt_width,), jnp.float32)
    for step_num in range(ITERS):
        col_scores = (pot_src[:, None] - cost_tile) / EPS + log_mass_a[:, None]
        col_peak, col_total = column_lse(col_scores)
        pot_tgt = -shrink * EPS * (col_peak + jnp.log(col_total))
        row_scores = (pot_tgt[None, :] - cost_tile) / EPS + log_mass_b[None, :]
        row_peak, row_total = row_lse(row_scores)
        pot_src = -shrink * EPS * (row_peak + jnp.log(row_total))
    weights = (jnp.exp(row_scores - row_peak[:, None]) / row_total[:, None]).astype(jnp.bfloat16)
    handed = jnp.where(
        is_last, final_fates.astype(jnp.bfloat16), jnp.zeros(final_fates.shape, jnp.bfloat16)
    )
    fate_maps = jnp.zeros((final_fates.shape[0], share_width), jnp.float32)
    for section_num in range(pair_count):
        active = pair_count - 1 - section_num
        partial_value = lax.dot_general(
            handed, weights, (((1,), (1,)), ((), ())), preferred_element_type=jnp.float32
        )
        fate_share = lax.psum_scatter(partial_value, "tgt", scatter_dimension=1, tiled=True)
        fate_share = jnp.where(live_share[None, :], fate_share, 0.0)
        fate_maps = jnp.where(pair_rank == active, fate_share, fate_maps)
        if section_num + 1 < pair_count:
            passed = shifted(fate_share.astype(jnp.bfloat16), "pair", -1)
            gathered = lax.all_gather(passed, ("src", "tgt"), axis=1, tiled=True)
            fresh = lax.dynamic_slice_in_dim(gathered, tgt_rank * tgt_width, tgt_width, 1)
            handed = jnp.where(pair_rank == active - 1, fresh, handed)
    return (fate_maps[None], pot_src[None])


def solution(mesh):
    placed = (P("pair", None, "src"), P(None, "tgt"), P("pair", "src"), P(), P(None, "tgt"))
    return jax.shard_map(
        local,
        mesh=mesh,
        in_specs=placed,
        out_specs=(P("pair", None, ("src", "tgt")), P("pair", "src")),
        check_vma=False,
    )
```

profile of v0, /device:TPU:0, one launch (start us, length us, event | category | flops | bytes accessed | tf_op | source)
XLA Modules:
  0.0 468.3 jit_solution(16337164708790287307)
XLA Ops:
  14.0 5.5 %collective-permute-done = f32[30,2048]{1,0:T(8,128)S(1)} collective-permute-done((f32[30,2048]{1,0:T(8,128)S(1)}, f32[30,2048]{1,0:T(8,128)S(1)}, u32[]{:S(2)}, u32[]{:S(2)}) %collective-permute-start) | collective-permute-done | bytes 245792 | tf_op jit(solution)/shard_map/ppermute | solution.py:25
  21.6 22.5 %all-reduce.2.cloned.1.call-done = f32[30,2048]{1,0:T(8,128)} async-done(((f32[30,2048]{1,0:T(8,128)}), f32[30,2048]{1,0:T(8,128)}) %all-reduce.2.cloned.1.call-update) | async-done | bytes 245776 | tf_op jit(solution)/shard_map/psum | solution.py:30
  45.0 10.0 %fusion.1 = (f32[1024]{0:T(1024)S(1)}, f32[2048,1024]{0,1:T(8,128)S(1)}) fusion(f32[2048]{0:T(1024)S(1)} %fusion.23, f32[1,30,2048]{2,0,1:T(1,128)} %param.21, f32[30,1024]{1,0:T(8,128)} %param.22, f32[30,2048]{1,0:T(8,128)} %all-reduce.2.cloned.1.call-done, s32[]{:T(128)S(6)} %select_n.247, pred[]{:T(512)S(6)} %eq.24, f32[1024]{0:T(1024)S(1)} %multiply_reduce_fusion.1, ...), kind=kOutput, calls=%fused_computation.59 | convolution fusion | flops 771781632 | bytes 8921093 | tf_op jit(solution)/shard_map/dot_general | solution.py:71
  70.1 5.2 %all-gather.2 = f32[8192]{0:T(1024)S(1)} all-gather(f32[2048]{0:T(1024)S(1)} %fusion.2), channel_id=4, replica_groups=mesh['pair'=4,'src'=2,'tgt'=4] {'tgt'}, dimensions={0}, use_global_device_ids=true | all-gather | bytes 40960 | tf_op jit(solution)/shard_map/all_gather | solution.py:13
  75.3 5.2 %all-gather.3 = f32[8192]{0:T(1024)S(1)} all-gather(f32[2048]{0:T(1024)S(1)} %exponential_reduce_fusion.14), channel_id=5, replica_groups=mesh['pair'=4,'src'=2,'tgt'=4] {'tgt'}, dimensions={0}, use_global_device_ids=true | all-gather | bytes 40960 | tf_op jit(solution)/shard_map/all_gather | solution.py:13
  101.3 5.2 %all-gather.6 = f32[8192]{0:T(1024)S(1)} all-gather(f32[2048]{0:T(1024)S(1)} %fusion.4), channel_id=8, replica_groups=mesh['pair'=4,'src'=2,'tgt'=4] {'tgt'}, dimensions={0}, use_global_device_ids=true | all-gather | bytes 40960 | tf_op jit(solution)/shard_map/all_gather | solution.py:13
  106.5 5.2 %all-gather.7 = f32[8192]{0:T(1024)S(1)} all-gather(f32[2048]{0:T(1024)S(1)} %exponential_reduce_fusion.12), channel_id=9, replica_groups=mesh['pair'=4,'src'=2,'tgt'=4] {'tgt'}, dimensions={0}, use_global_device_ids=true | all-gather | bytes 40960 | tf_op jit(solution)/shard_map/all_gather | solution.py:13
  116.7 5.3 %exponential_reduce_fusion.11 = f32[1024]{0:T(1024)S(1)} fusion(f32[2048,1024]{0,1:T(8,128)} %copy-done, f32[1024]{0:T(1024)S(1)} %fusion.5, f32[2048]{0:T(1024)S(1)} %add_multiply_fusion.6, f32[2048]{0:T(1024)S(1)} %fusion.23), kind=kLoop, calls=%fused_computation.49 | loop fusion | flops 10484736 | bytes 8413184 | tf_op jit(solution)/shard_map/reduce_sum | solution.py:40
  134.7 5.2 %all-gather.10 = f32[8192]{0:T(1024)S(1)} all-gather(f32[2048]{0:T(1024)S(1)} %fusion.6), channel_id=12, replica_groups=mesh['pair'=4,'src'=2,'tgt'=4] {'tgt'}, dimensions={0}, use_global_device_ids=true | all-gather | bytes 40960 | tf_op jit(solution)/shard_map/all_gather | solution.py:13
  139.9 5.2 %all-gather.11 = f32[8192]{0:T(1024)S(1)} all-gather(f32[2048]{0:T(1024)S(1)} %exponential_reduce_fusion.10), channel_id=13, replica_groups=mesh['pair'=4,'src'=2,'tgt'=4] {'tgt'}, dimensions={0}, use_global_device_ids=true | all-gather | bytes 40960 | tf_op jit(solution)/shard_map/all_gather | solution.py:13
  150.1 5.3 %exponential_reduce_fusion.9 = f32[1024]{0:T(1024)S(1)} fusion(f32[2048,1024]{0,1:T(8,128)} %copy-done, f32[1024]{0:T(1024)S(1)} %fusion.7, f32[2048]{0:T(1024)S(1)} %add_multiply_fusion.5, f32[2048]{0:T(1024)S(1)} %fusion.23), kind=kLoop, calls=%fused_computation.45 | loop fusion | flops 10484736 | bytes 8413184 | tf_op jit(solution)/shard_map/reduce_sum | solution.py:40
  167.8 5.2 %all-gather.14 = f32[8192]{0:T(1024)S(1)} all-gather(f32[2048]{0:T(1024)S(1)} %fusion.8), channel_id=16, replica_groups=mesh['pair'=4,'src'=2,'tgt'=4] {'tgt'}, dimensions={0}, use_global_device_ids=true | all-gather | bytes 40960 | tf_op jit(solution)/shard_map/all_gather | solution.py:13
  173.1 5.2 %all-gather.15 = f32[8192]{0:T(1024)S(1)} all-gather(f32[2048]{0:T(1024)S(1)} %exponential_reduce_fusion.8), channel_id=17, replica_groups=mesh['pair'=4,'src'=2,'tgt'=4] {'tgt'}, dimensions={0}, use_global_device_ids=true | all-gather | bytes 40960 | tf_op jit(solution)/shard_map/all_gather | solution.py:13
  183.2 5.3 %exponential_reduce_fusion.7 = f32[1024]{0:T(1024)S(1)} fusion(f32[2048,1024]{0,1:T(8,128)} %copy-done, f32[1024]{0:T(1024)S(1)} %fusion.9, f32[2048]{0:T(1024)S(1)} %add_multiply_fusion.4, f32[2048]{0:T(1024)S(1)} %fusion.23), kind=kLoop, calls=%fused_computation.41 | loop fusion | flops 10484736 | bytes 8413184 | tf_op jit(solution)/shard_map/reduce_sum | solution.py:40
  201.4 5.2 %all-gather.18 = f32[8192]{0:T(1024)S(1)} all-gather(f32[2048]{0:T(1024)S(1)} %fusion.10), channel_id=20, replica_groups=mesh['pair'=4,'src'=2,'tgt'=4] {'tgt'}, dimensions={0}, use_global_device_ids=true | all-gather | bytes 40960 | tf_op jit(solution)/shard_map/all_gather | solution.py:13
  206.6 5.2 %all-gather.19 = f32[8192]{0:T(1024)S(1)} all-gather(f32[2048]{0:T(1024)S(1)} %exponential_reduce_fusion.6), channel_id=21, replica_groups=mesh['pair'=4,'src'=2,'tgt'=4] {'tgt'}, dimensions={0}, use_global_device_ids=true | all-gather | bytes 40960 | tf_op jit(solution)/shard_map/all_gather | solution.py:13
  216.8 5.3 %exponential_reduce_fusion.5 = f32[1024]{0:T(1024)S(1)} fusion(f32[2048,1024]{0,1:T(8,128)} %copy-done, f32[1024]{0:T(1024)S(1)} %fusion.11, f32[2048]{0:T(1024)S(1)} %add_multiply_fusion.3, f32[2048]{0:T(1024)S(1)} %fusion.23), kind=kLoop, calls=%fused_computation.37 | loop fusion | flops 10484736 | bytes 8413184 | tf_op jit(solution)/shard_map/reduce_sum | solution.py:40
  234.6 5.2 %all-gather.22 = f32[8192]{0:T(1024)S(1)} all-gather(f32[2048]{0:T(1024)S(1)} %fusion.12), channel_id=24, replica_groups=mesh['pair'=4,'src'=2,'tgt'=4] {'tgt'}, dimensions={0}, use_global_device_ids=true | all-gather | bytes 40960 | tf_op jit(solution)/shard_map/all_gather | solution.py:13
  239.8 5.2 %all-gather.23 = f32[8192]{0:T(1024)S(1)} all-gather(f32[2048]{0:T(1024)S(1)} %exponential_reduce_fusion.4), channel_id=25, replica_groups=mesh['pair'=4,'src'=2,'tgt'=4] {'tgt'}, dimensions={0}, use_global_device_ids=true | all-gather | bytes 40960 | tf_op jit(solution)/shard_map/all_gather | solution.py:13
  250.0 5.3 %exponential_reduce_fusion.3 = f32[1024]{0:T(1024)S(1)} fusion(f32[2048,1024]{0,1:T(8,128)} %copy-done, f32[1024]{0:T(1024)S(1)} %fusion.13, f32[2048]{0:T(1024)S(1)} %add_multiply_fusion.2, f32[2048]{0:T(1024)S(1)} %fusion.23), kind=kLoop, calls=%fused_computation.33 | loop fusion | flops 10484736 | bytes 8413184 | tf_op jit(solution)/shard_map/reduce_sum | solution.py:40
  267.9 5.2 %all-gather.26 = f32[8192]{0:T(1024)S(1)} all-gather(f32[2048]{0:T(1024)S(1)} %fusion.14), channel_id=28, replica_groups=mesh['pair'=4,'src'=2,'tgt'=4] {'tgt'}, dimensions={0}, use_global_device_ids=true | all-gather | bytes 40960 | tf_op jit(solution)/shard_map/all_gather | solution.py:13
  273.1 5.2 %all-gather.27 = f32[8192]{0:T(1024)S(1)} all-gather(f32[2048]{0:T(1024)S(1)} %exponential_reduce_fusion.2), channel_id=29, replica_groups=mesh['pair'=4,'src'=2,'tgt'=4] {'tgt'}, dimensions={0}, use_global_device_ids=true | all-gather | bytes 40960 | tf_op jit(solution)/shard_map/all_gather | solution.py:13
  283.3 5.3 %exponential_reduce_fusion.1 = f32[1024]{0:T(1024)S(1)} fusion(f32[2048,1024]{0,1:T(8,128)} %copy-done, f32[1024]{0:T(1024)S(1)} %fusion.15, f32[2048]{0:T(1024)S(1)} %add_multiply_fusion.1, f32[2048]{0:T(1024)S(1)} %fusion.23), kind=kLoop, calls=%fused_computation.29 | loop fusion | flops 10484736 | bytes 8413184 | tf_op jit(solution)/shard_map/reduce_sum | solution.py:40
  301.1 5.3 %all-gather.30 = f32[8192]{0:T(1024)S(1)} all-gather(f32[2048]{0:T(1024)S(1)} %fusion.16), channel_id=32, replica_groups=mesh['pair'=4,'src'=2,'tgt'=4] {'tgt'}, dimensions={0}, use_global_device_ids=true | all-gather | bytes 40960 | tf_op jit(solution)/shard_map/all_gather | solution.py:13
  306.4 5.2 %all-gather.31 = f32[8192]{0:T(1024)S(1)} all-gather(f32[2048]{0:T(1024)S(1)} %exponential_reduce_fusion), channel_id=33, replica_groups=mesh['pair'=4,'src'=2,'tgt'=4] {'tgt'}, dimensions={0}, use_global_device_ids=true | all-gather | bytes 40960 | tf_op jit(solution)/shard_map/all_gather | solution.py:13
  320.7 20.0 %reduce-scatter.5.cloned.1.call-done = f32[40,512]{1,0:T(8,128)} async-done(((f32[40,2048]{1,0:T(8,128)}), f32[40,512]{1,0:T(8,128)}) %reduce-scatter.5.cloned.1.call-update) | async-done | bytes 81936 | tf_op jit(solution)/shard_map/reduce_scatter | solution.py:116
  347.7 9.4 %all_gather.265 = bf16[40,4096]{1,0:T(8,128)(2,1)S(1)} all-gather(bf16[40,512]{1,0:T(8,128)(2,1)S(1)} %collective-permute-done.1), channel_id=1, replica_groups=mesh['pair'=4,'src'=2,'tgt'=4] {'src','tgt'}, dimensions={1}, use_global_device_ids=true | all-gather | bytes 368640 | tf_op jit(solution)/shard_map/all_gather | solution.py:121
  360.9 19.6 %reduce-scatter.7.cloned.1.call-done = f32[40,512]{1,0:T(8,128)} async-done(((f32[40,2048]{1,0:T(8,128)}), f32[40,512]{1,0:T(8,128)}) %reduce-scatter.7.cloned.1.call-update) | async-done | bytes 81936 | tf_op jit(solution)/shard_map/reduce_scatter | solution.py:116
  387.3 9.6 %all_gather.266 = bf16[40,4096]{1,0:T(8,128)(2,1)S(1)} all-gather(bf16[40,512]{1,0:T(8,128)(2,1)S(1)} %collective-permute-done.2), channel_id=1, replica_groups=mesh['pair'=4,'src'=2,'tgt'=4] {'src','tgt'}, dimensions={1}, use_global_device_ids=true | all-gather | bytes 368640 | tf_op jit(solution)/shard_map/all_gather | solution.py:121
  400.7 19.6 %reduce-scatter.9.cloned.1.call-done = f32[40,512]{1,0:T(8,128)} async-done(((f32[40,2048]{1,0:T(8,128)}), f32[40,512]{1,0:T(8,128)}) %reduce-scatter.9.cloned.1.call-update) | async-done | bytes 81936 | tf_op jit(solution)/shard_map/reduce_scatter | solution.py:116
  427.1 9.4 %all_gather.267 = bf16[40,4096]{1,0:T(8,128)(2,1)S(1)} all-gather(bf16[40,512]{1,0:T(8,128)(2,1)S(1)} %collective-permute-done.3), channel_id=1, replica_groups=mesh['pair'=4,'src'=2,'tgt'=4] {'src','tgt'}, dimensions={1}, use_global_device_ids=true | all-gather | bytes 368640 | tf_op jit(solution)/shard_map/all_gather | solution.py:121
  440.9 19.1 %reduce-scatter.11.cloned.1.call-done = f32[40,512]{1,0:T(8,128)} async-done(((f32[40,2048]{1,0:T(8,128)}), f32[40,512]{1,0:T(8,128)}) %reduce-scatter.11.cloned.1.call-update) | async-done | bytes 81936 | tf_op jit(solution)/shard_map/reduce_scatter | solution.py:116
  (239 shorter events, 193.2 us)
Async XLA Ops:
  7.2 36.9 %all-reduce.2.cloned.1.call-start = ((), (), s32[]{:S(2)}) async-start(), calls=%async_computation.4 | async-start | bytes 524288 | tf_op jit(solution)/shard_map/psum | solution.py:30
  8.2 11.3 %collective-permute-start = (f32[30,2048]{1,0:T(8,128)S(1)}, f32[30,2048]{1,0:T(8,128)S(1)}, u32[]{:S(2)}, u32[]{:S(2)}) collective-permute-start(f32[30,2048]{1,0:T(8,128)S(1)} %bitcast.139), channel_id=1, source_target_pairs={{8,0},{16,8},{24,16},{9,1},{17,9},{25,17},{10,2},{18,10},{26,18},{... | collective-permute-start | bytes 737288 | tf_op jit(solution)/shard_map/ppermute | solution.py:25
  20.2 320.5 %reduce-scatter.5.cloned.1.call-start = ((), (), s32[]{:S(2)}) async-start(), calls=%async_computation.5 | async-start | bytes 409600 | tf_op jit(solution)/shard_map/reduce_scatter | solution.py:116
  55.0 12.8 %copy-start = (f32[2048,1024]{0,1:T(8,128)}, f32[2048,1024]{0,1:T(8,128)S(1)}, u32[]{:S(2)}) copy-start(f32[2048,1024]{0,1:T(8,128)S(1)} %get-tuple-element.1373) | copy-start | bytes 25165828
  80.7 5.8 %copy-start.1 = (f32[2048,1024]{0,1:T(8,128)S(1)}, f32[2048,1024]{0,1:T(8,128)}, u32[]{:S(2)}) copy-start(f32[2048,1024]{0,1:T(8,128)} %copy-done) | copy-start | bytes 25165828
  111.9 19.1 %slice-start = ((s8[8388608]{0:T(1024)(128)(4,1)}), s8[4194304]{0:T(1024)(128)(4,1)S(1)}, s32[]{:S(2)}) async-start(s8[8388608]{0:T(1024)(128)(4,1)} %bitcast.111), calls=%async_computation.9 | async-start | bytes 8388608
  116.7 14.3 %slice-start.1 = ((s8[8388608]{0:T(1024)(128)(4,1)}), s8[4194304]{0:T(1024)(128)(4,1)S(1)}, s32[]{:S(2)}) async-start(s8[8388608]{0:T(1024)(128)(4,1)} %bitcast.111), calls=%async_computation.10 | async-start | bytes 8388608
  145.3 18.9 %slice-start.2 = ((s8[8388608]{0:T(1024)(128)(4,1)}), s8[4194304]{0:T(1024)(128)(4,1)S(1)}, s32[]{:S(2)}) async-start(s8[8388608]{0:T(1024)(128)(4,1)} %bitcast.113), calls=%async_computation.11 | async-start | bytes 8388608
  150.1 14.1 %slice-start.3 = ((s8[8388608]{0:T(1024)(128)(4,1)}), s8[4194304]{0:T(1024)(128)(4,1)S(1)}, s32[]{:S(2)}) async-start(s8[8388608]{0:T(1024)(128)(4,1)} %bitcast.113), calls=%async_computation.12 | async-start | bytes 8388608
  178.5 19.3 %slice-start.4 = ((s8[8388608]{0:T(1024)(128)(4,1)}), s8[4194304]{0:T(1024)(128)(4,1)S(1)}, s32[]{:S(2)}) async-start(s8[8388608]{0:T(1024)(128)(4,1)} %bitcast.115), calls=%async_computation.13 | async-start | bytes 8388608
  183.2 14.5 %slice-start.5 = ((s8[8388608]{0:T(1024)(128)(4,1)}), s8[4194304]{0:T(1024)(128)(4,1)S(1)}, s32[]{:S(2)}) async-start(s8[8388608]{0:T(1024)(128)(4,1)} %bitcast.115), calls=%async_computation.14 | async-start | bytes 8388608
  212.1 18.9 %slice-start.6 = ((s8[8388608]{0:T(1024)(128)(4,1)}), s8[4194304]{0:T(1024)(128)(4,1)S(1)}, s32[]{:S(2)}) async-start(s8[8388608]{0:T(1024)(128)(4,1)} %bitcast.117), calls=%async_computation.15 | async-start | bytes 8388608
  216.8 14.1 %slice-start.7 = ((s8[8388608]{0:T(1024)(128)(4,1)}), s8[4194304]{0:T(1024)(128)(4,1)S(1)}, s32[]{:S(2)}) async-start(s8[8388608]{0:T(1024)(128)(4,1)} %bitcast.117), calls=%async_computation.16 | async-start | bytes 8388608
  245.2 19.0 %slice-start.8 = ((s8[8388608]{0:T(1024)(128)(4,1)}), s8[4194304]{0:T(1024)(128)(4,1)S(1)}, s32[]{:S(2)}) async-start(s8[8388608]{0:T(1024)(128)(4,1)} %bitcast.119), calls=%async_computation.17 | async-start | bytes 8388608
  250.0 14.3 %slice-start.9 = ((s8[8388608]{0:T(1024)(128)(4,1)}), s8[4194304]{0:T(1024)(128)(4,1)S(1)}, s32[]{:S(2)}) async-start(s8[8388608]{0:T(1024)(128)(4,1)} %bitcast.119), calls=%async_computation.18 | async-start | bytes 8388608
  278.6 18.9 %slice-start.10 = ((s8[8388608]{0:T(1024)(128)(4,1)}), s8[4194304]{0:T(1024)(128)(4,1)S(1)}, s32[]{:S(2)}) async-start(s8[8388608]{0:T(1024)(128)(4,1)} %bitcast.121), calls=%async_computation.19 | async-start | bytes 8388608
  283.3 14.1 %slice-start.11 = ((s8[8388608]{0:T(1024)(128)(4,1)}), s8[4194304]{0:T(1024)(128)(4,1)S(1)}, s32[]{:S(2)}) async-start(s8[8388608]{0:T(1024)(128)(4,1)} %bitcast.121), calls=%async_computation.20 | async-start | bytes 8388608
  301.1 17.3 %copy-start.3 = (f32[40,1024]{1,0:T(8,128)S(1)}, f32[40,1024]{1,0:T(8,128)}, u32[]{:S(2)}) copy-start(f32[40,1024]{1,0:T(8,128)} %param.25) | copy-start | bytes 491524
  316.5 1.9 copy-start.2
  320.0 60.5 %reduce-scatter.7.cloned.1.call-start = ((), (), s32[]{:S(2)}) async-start(), calls=%async_computation.6 | async-start | bytes 409600 | tf_op jit(solution)/shard_map/reduce_scatter | solution.py:116
  341.6 118.3 %copy-start.4 = (f32[40,512]{1,0:T(8,128)S(1)}, f32[40,512]{1,0:T(8,128)}, u32[]{:S(2)}) copy-start(f32[40,512]{1,0:T(8,128)} %reduce-scatter.5.cloned.1.call-done) | copy-start | bytes 245764
  341.6 6.0 %collective-permute-start.1 = (bf16[40,512]{1,0:T(8,128)(2,1)S(1)}, bf16[40,512]{1,0:T(8,128)(2,1)S(1)}, u32[]{:S(2)}, u32[]{:S(2)}) collective-permute-start(bf16[40,512]{1,0:T(8,128)(2,1)S(1)} %select_convert_fusion.2), channel_id=1, source_target_pairs={{8,0},{16,8},{24,16},{9,1},{17,9},{25,17},{10,2},{18,10},{26,18},{... | collective-permute-start | bytes 122888 | tf_op jit(solution)/shard_map/ppermute | solution.py:25
  360.8 59.5 %reduce-scatter.9.cloned.1.call-start = ((), (), s32[]{:S(2)}) async-start(), calls=%async_computation.7 | async-start | bytes 409600 | tf_op jit(solution)/shard_map/reduce_scatter | solution.py:116
  380.4 79.5 %copy-start.5 = (f32[40,512]{1,0:T(8,128)S(1)}, f32[40,512]{1,0:T(8,128)}, u32[]{:S(2)}) copy-start(f32[40,512]{1,0:T(8,128)} %reduce-scatter.7.cloned.1.call-done) | copy-start | bytes 245764
  381.4 5.9 %collective-permute-start.2 = (bf16[40,512]{1,0:T(8,128)(2,1)S(1)}, bf16[40,512]{1,0:T(8,128)(2,1)S(1)}, u32[]{:S(2)}, u32[]{:S(2)}) collective-permute-start(bf16[40,512]{1,0:T(8,128)(2,1)S(1)} %select_convert_fusion.1), channel_id=1, source_target_pairs={{8,0},{16,8},{24,16},{9,1},{17,9},{25,17},{10,2},{18,10},{26,18},{... | collective-permute-start | bytes 122888 | tf_op jit(solution)/shard_map/ppermute | solution.py:25
  400.7 59.2 %reduce-scatter.11.cloned.1.call-start = ((), (), s32[]{:S(2)}) async-start(), calls=%async_computation.8 | async-start | bytes 409600 | tf_op jit(solution)/shard_map/reduce_scatter | solution.py:116
  421.2 5.9 %collective-permute-start.3 = (bf16[40,512]{1,0:T(8,128)(2,1)S(1)}, bf16[40,512]{1,0:T(8,128)(2,1)S(1)}, u32[]{:S(2)}, u32[]{:S(2)}) collective-permute-start(bf16[40,512]{1,0:T(8,128)(2,1)S(1)} %select_convert_fusion), channel_id=1, source_target_pairs={{8,0},{16,8},{24,16},{9,1},{17,9},{25,17},{10,2},{18,10},{26,18},{... | collective-permute-start | bytes 122888 | tf_op jit(solution)/shard_map/ppermute | solution.py:25
Sparse Core Ops, SparseCore 0:
  20.4 23.6 all-reduce.1
  320.1 20.5 reduce-scatter.4
  361.0 19.4 reduce-scatter.6
  400.8 19.4 reduce-scatter.8
  440.4 19.4 reduce-scatter.10
where the time goes:
time: 477 us; the launch traced here: 468 us
  blocking collectives  182 us (38%)
  waiting for transfers between devices  120 us (25%)
  other arithmetic  115 us (24%)
  matrix products  22.8 us (5%)
  between operations  16.2 us (3%)
  local copies, waits for them, and re-layouts  6.12 us (1%)
  starting transfers between devices  5.5 us (1%)
    all_gather x32, blocking collectives, joined(): everything = jax.tree.map(lambda part: lax.all_gather(part, axis), shard)  154 us
    reduce_scatter x4, waiting for transfers between devices, local(): lax.psum_scatter(partial_value, 'tgt', scatter_dimension=1, tiled=True)  78.2 us
    reduce_sum x8, other arithmetic, column_lse(): totals = jnp.sum(jnp.exp(col_scores - peak[None, :]), axis=0)  37 us
    reduce_max x7, other arithmetic, column_lse(): peak = jnp.max(col_scores, axis=0)  33.1 us
    all_gather x3, blocking collectives, local(): gathered = lax.all_gather(passed, ('src', 'tgt'), axis=1, tiled=True)  28.4 us
    psum x1, waiting for transfers between devices, from_root(): return lax.psum(jnp.where(mine, shard, jnp.zeros_like(shard)), axis)  22.5 us
    ppermute x4, waiting for transfers between devices, shifted(): return lax.ppermute(shard, axis, pairs)  19.2 us
    reduce_sum x8, other arithmetic, row_lse(): totals = jnp.sum(jnp.exp(row_scores - peak[:, None]), axis=1)  17.8 us
  transfers between devices with their start and end apart: 9, of which 9 were waited for; matrix products, arithmetic and copies ran while one was open for 1% of the time, Pallas kernels for 0%

commit v1 on v0

--- a/solution.py
+++ b/solution.py
@@ -27,7 +27,7 @@
 
 def from_root(shard, axis, root):
     mine = lax.axis_index(axis) == root
-    return lax.psum(jnp.where(mine, shard, jnp.zeros_like(shard)), axis)
+    return jnp.sum(lax.all_gather(jnp.where(mine, shard, jnp.zeros_like(shard)), axis), axis=0)
 
 
 def combine(first, second):

time: 477 us -> 461 us (0.966)
  waiting for transfers between devices: 120 us -> 97 us
  blocking collectives: 182 us -> 190 us
    psum x1 -> x0, waiting for transfers between devices: 22.5 us -> none  [from_root(): return lax.psum(jnp.where(mine, shard, jnp.zeros_like(shard)), axis)]
    all_gather x0 -> x1, blocking collectives: none -> 8.13 us  [from_root(): lax.all_gather(jnp.where(mine, shard, jnp.zeros_like(shard)), axis)]
  transfers between devices with their start and end apart: 9 -> 8, of which waited for: 9 -> 8; matrix products, arithmetic and copies ran while one was open for 1% -> 1% of each run, Pallas kernels for 0% -> 0%
where the time goes in v1:
time: 461 us; the launch traced here: 452 us
  blocking collectives  190 us (41%)
  other arithmetic  113 us (25%)
  waiting for transfers between devices  97 us (21%)
  matrix products  22.7 us (5%)
  between operations  16.2 us (4%)
  local copies, waits for them, and re-layouts  6.11 us (1%)
  starting transfers between devices  5.45 us (1%)
    all_gather x32, blocking collectives, joined(): everything = jax.tree.map(lambda part: lax.all_gather(part, axis), shard)  154 us
    reduce_scatter x4, waiting for transfers between devices, local(): lax.psum_scatter(partial_value, 'tgt', scatter_dimension=1, tiled=True)  79 us
    reduce_sum x8, other arithmetic, column_lse(): totals = jnp.sum(jnp.exp(col_scores - peak[None, :]), axis=0)  37 us
    reduce_max x7, other arithmetic, column_lse(): peak = jnp.max(col_scores, axis=0)  33.2 us
    all_gather x3, blocking collectives, local(): gathered = lax.all_gather(passed, ('src', 'tgt'), axis=1, tiled=True)  28.4 us
    ppermute x4, waiting for transfers between devices, shifted(): return lax.ppermute(shard, axis, pairs)  17.9 us
    reduce_sum x8, other arithmetic, row_lse(): totals = jnp.sum(jnp.exp(row_scores - peak[:, None]), axis=1)  17.9 us
    dot_general x4, matrix products, local(): lax.dot_general(handed, weights, (((1,), (1,)), ((), ())), preferred_elem...  12.8 us
  transfers between devices with their start and end apart: 8, of which 8 were waited for; matrix products, arithmetic and copies ran while one was open for 1% of the time, Pallas kernels for 0%

profile of v1, /device:TPU:0, one launch (start us, length us, event | category | flops | bytes accessed | tf_op | source)
XLA Modules:
  0.0 451.9 jit_solution(15774652557234006693)
XLA Ops:
  19.5 8.1 %all-gather.33 = f32[2,30,2048]{2,1,0:T(8,128)S(1)} all-gather(f32[1,30,2048]{2,1,0:T(8,128)S(1)} %select_bitcast_fusion), channel_id=2, replica_groups=mesh['pair'=4,'src'=2,'tgt'=4] {'src'}, dimensions={0}, use_global_device_ids=true | all-gather | bytes 737280 | tf_op jit(solution)/shard_map/all_gather | solution.py:30
  27.7 9.9 %fusion.1 = (f32[1024]{0:T(1024)S(1)}, f32[2048,1024]{0,1:T(8,128)S(1)}) fusion(f32[2048]{0:T(1024)S(1)} %fusion.23, f32[1,30,2048]{2,0,1:T(1,128)} %param.21, f32[30,1024]{1,0:T(8,128)} %param.22, f32[30,2048]{1,0:T(8,128)S(1)} %reduce_sum.172, s32[]{:T(128)S(6)} %select_n.247, pred[]{:T(512)S(6)} %eq.24, f32[1024]{0:T(1024)S(1)} %multiply_reduce_fusion.1, ...), kind=kOutput, calls=%fused_computation.59 | convolution fusion | flops 771781632 | bytes 8912901 | tf_op jit(solution)/shard_map/dot_general | solution.py:71
  52.7 5.2 %all-gather.3 = f32[8192]{0:T(1024)S(1)} all-gather(f32[2048]{0:T(1024)S(1)} %fusion.2), channel_id=5, replica_groups=mesh['pair'=4,'src'=2,'tgt'=4] {'tgt'}, dimensions={0}, use_global_device_ids=true | all-gather | bytes 40960 | tf_op jit(solution)/shard_map/all_gather | solution.py:13
  57.9 5.2 %all-gather.4 = f32[8192]{0:T(1024)S(1)} all-gather(f32[2048]{0:T(1024)S(1)} %exponential_reduce_fusion.14), channel_id=6, replica_groups=mesh['pair'=4,'src'=2,'tgt'=4] {'tgt'}, dimensions={0}, use_global_device_ids=true | all-gather | bytes 40960 | tf_op jit(solution)/shard_map/all_gather | solution.py:13
  84.0 5.2 %all-gather.7 = f32[8192]{0:T(1024)S(1)} all-gather(f32[2048]{0:T(1024)S(1)} %fusion.4), channel_id=9, replica_groups=mesh['pair'=4,'src'=2,'tgt'=4] {'tgt'}, dimensions={0}, use_global_device_ids=true | all-gather | bytes 40960 | tf_op jit(solution)/shard_map/all_gather | solution.py:13
  89.2 5.2 %all-gather.8 = f32[8192]{0:T(1024)S(1)} all-gather(f32[2048]{0:T(1024)S(1)} %exponential_reduce_fusion.12), channel_id=10, replica_groups=mesh['pair'=4,'src'=2,'tgt'=4] {'tgt'}, dimensions={0}, use_global_device_ids=true | all-gather | bytes 40960 | tf_op jit(solution)/shard_map/all_gather | solution.py:13
  99.4 5.3 %exponential_reduce_fusion.11 = f32[1024]{0:T(1024)S(1)} fusion(f32[2048,1024]{0,1:T(8,128)} %copy-done, f32[1024]{0:T(1024)S(1)} %fusion.5, f32[2048]{0:T(1024)S(1)} %add_multiply_fusion.6, f32[2048]{0:T(1024)S(1)} %fusion.23), kind=kLoop, calls=%fused_computation.49 | loop fusion | flops 10484736 | bytes 8413184 | tf_op jit(solution)/shard_map/reduce_sum | solution.py:40
  117.4 5.2 %all-gather.11 = f32[8192]{0:T(1024)S(1)} all-gather(f32[2048]{0:T(1024)S(1)} %fusion.6), channel_id=13, replica_groups=mesh['pair'=4,'src'=2,'tgt'=4] {'tgt'}, dimensions={0}, use_global_device_ids=true | all-gather | bytes 40960 | tf_op jit(solution)/shard_map/all_gather | solution.py:13
  122.6 5.2 %all-gather.12 = f32[8192]{0:T(1024)S(1)} all-gather(f32[2048]{0:T(1024)S(1)} %exponential_reduce_fusion.10), channel_id=14, replica_groups=mesh['pair'=4,'src'=2,'tgt'=4] {'tgt'}, dimensions={0}, use_global_device_ids=true | all-gather | bytes 40960 | tf_op jit(solution)/shard_map/all_gather | solution.py:13
  132.8 5.3 %exponential_reduce_fusion.9 = f32[1024]{0:T(1024)S(1)} fusion(f32[2048,1024]{0,1:T(8,128)} %copy-done, f32[1024]{0:T(1024)S(1)} %fusion.7, f32[2048]{0:T(1024)S(1)} %add_multiply_fusion.5, f32[2048]{0:T(1024)S(1)} %fusion.23), kind=kLoop, calls=%fused_computation.45 | loop fusion | flops 10484736 | bytes 8413184 | tf_op jit(solution)/shard_map/reduce_sum | solution.py:40
  150.6 5.2 %all-gather.15 = f32[8192]{0:T(1024)S(1)} all-gather(f32[2048]{0:T(1024)S(1)} %fusion.8), channel_id=17, replica_groups=mesh['pair'=4,'src'=2,'tgt'=4] {'tgt'}, dimensions={0}, use_global_device_ids=true | all-gather | bytes 40960 | tf_op jit(solution)/shard_map/all_gather | solution.py:13
  155.8 5.2 %all-gather.16 = f32[8192]{0:T(1024)S(1)} all-gather(f32[2048]{0:T(1024)S(1)} %exponential_reduce_fusion.8), channel_id=18, replica_groups=mesh['pair'=4,'src'=2,'tgt'=4] {'tgt'}, dimensions={0}, use_global_device_ids=true | all-gather | bytes 40960 | tf_op jit(solution)/shard_map/all_gather | solution.py:13
  166.0 5.3 %exponential_reduce_fusion.7 = f32[1024]{0:T(1024)S(1)} fusion(f32[2048,1024]{0,1:T(8,128)} %copy-done, f32[1024]{0:T(1024)S(1)} %fusion.9, f32[2048]{0:T(1024)S(1)} %add_multiply_fusion.4, f32[2048]{0:T(1024)S(1)} %fusion.23), kind=kLoop, calls=%fused_computation.41 | loop fusion | flops 10484736 | bytes 8413184 | tf_op jit(solution)/shard_map/reduce_sum | solution.py:40
  175.7 4.8 %all-gather.18 = f32[2048]{0:T(1024)S(1)} all-gather(f32[1024]{0:T(1024)S(1)} %exponential_reduce_fusion.7), channel_id=20, replica_groups=mesh['pair'=4,'src'=2,'tgt'=4] {'src'}, dimensions={0}, use_global_device_ids=true | all-gather | bytes 12288 | tf_op jit(solution)/shard_map/all_gather | solution.py:13
  184.2 5.2 %all-gather.19 = f32[8192]{0:T(1024)S(1)} all-gather(f32[2048]{0:T(1024)S(1)} %fusion.10), channel_id=21, replica_groups=mesh['pair'=4,'src'=2,'tgt'=4] {'tgt'}, dimensions={0}, use_global_device_ids=true | all-gather | bytes 40960 | tf_op jit(solution)/shard_map/all_gather | solution.py:13
  189.4 5.2 %all-gather.20 = f32[8192]{0:T(1024)S(1)} all-gather(f32[2048]{0:T(1024)S(1)} %exponential_reduce_fusion.6), channel_id=22, replica_groups=mesh['pair'=4,'src'=2,'tgt'=4] {'tgt'}, dimensions={0}, use_global_device_ids=true | all-gather | bytes 40960 | tf_op jit(solution)/shard_map/all_gather | solution.py:13
  199.6 5.3 %exponential_reduce_fusion.5 = f32[1024]{0:T(1024)S(1)} fusion(f32[2048,1024]{0,1:T(8,128)} %copy-done, f32[1024]{0:T(1024)S(1)} %fusion.11, f32[2048]{0:T(1024)S(1)} %add_multiply_fusion.3, f32[2048]{0:T(1024)S(1)} %fusion.23), kind=kLoop, calls=%fused_computation.37 | loop fusion | flops 10484736 | bytes 8413184 | tf_op jit(solution)/shard_map/reduce_sum | solution.py:40
  217.4 5.2 %all-gather.23 = f32[8192]{0:T(1024)S(1)} all-gather(f32[2048]{0:T(1024)S(1)} %fusion.12), channel_id=25, replica_groups=mesh['pair'=4,'src'=2,'tgt'=4] {'tgt'}, dimensions={0}, use_global_device_ids=true | all-gather | bytes 40960 | tf_op jit(solution)/shard_map/all_gather | solution.py:13
  222.6 5.2 %all-gather.24 = f32[8192]{0:T(1024)S(1)} all-gather(f32[2048]{0:T(1024)S(1)} %exponential_reduce_fusion.4), channel_id=26, replica_groups=mesh['pair'=4,'src'=2,'tgt'=4] {'tgt'}, dimensions={0}, use_global_device_ids=true | all-gather | bytes 40960 | tf_op jit(solution)/shard_map/all_gather | solution.py:13
  232.8 5.3 %exponential_reduce_fusion.3 = f32[1024]{0:T(1024)S(1)} fusion(f32[2048,1024]{0,1:T(8,128)} %copy-done, f32[1024]{0:T(1024)S(1)} %fusion.13, f32[2048]{0:T(1024)S(1)} %add_multiply_fusion.2, f32[2048]{0:T(1024)S(1)} %fusion.23), kind=kLoop, calls=%fused_computation.33 | loop fusion | flops 10484736 | bytes 8413184 | tf_op jit(solution)/shard_map/reduce_sum | solution.py:40
  250.7 5.2 %all-gather.27 = f32[8192]{0:T(1024)S(1)} all-gather(f32[2048]{0:T(1024)S(1)} %fusion.14), channel_id=29, replica_groups=mesh['pair'=4,'src'=2,'tgt'=4] {'tgt'}, dimensions={0}, use_global_device_ids=true | all-gather | bytes 40960 | tf_op jit(solution)/shard_map/all_gather | solution.py:13
  255.9 5.2 %all-gather.28 = f32[8192]{0:T(1024)S(1)} all-gather(f32[2048]{0:T(1024)S(1)} %exponential_reduce_fusion.2), channel_id=30, replica_groups=mesh['pair'=4,'src'=2,'tgt'=4] {'tgt'}, dimensions={0}, use_global_device_ids=true | all-gather | bytes 40960 | tf_op jit(solution)/shard_map/all_gather | solution.py:13
  266.1 5.3 %exponential_reduce_fusion.1 = f32[1024]{0:T(1024)S(1)} fusion(f32[2048,1024]{0,1:T(8,128)} %copy-done, f32[1024]{0:T(1024)S(1)} %fusion.15, f32[2048]{0:T(1024)S(1)} %add_multiply_fusion.1, f32[2048]{0:T(1024)S(1)} %fusion.23), kind=kLoop, calls=%fused_computation.29 | loop fusion | flops 10484736 | bytes 8413184 | tf_op jit(solution)/shard_map/reduce_sum | solution.py:40
  283.9 5.3 %all-gather.31 = f32[8192]{0:T(1024)S(1)} all-gather(f32[2048]{0:T(1024)S(1)} %fusion.16), channel_id=33, replica_groups=mesh['pair'=4,'src'=2,'tgt'=4] {'tgt'}, dimensions={0}, use_global_device_ids=true | all-gather | bytes 40960 | tf_op jit(solution)/shard_map/all_gather | solution.py:13
  289.2 5.2 %all-gather.32 = f32[8192]{0:T(1024)S(1)} all-gather(f32[2048]{0:T(1024)S(1)} %exponential_reduce_fusion), channel_id=34, replica_groups=mesh['pair'=4,'src'=2,'tgt'=4] {'tgt'}, dimensions={0}, use_global_device_ids=true | all-gather | bytes 40960 | tf_op jit(solution)/shard_map/all_gather | solution.py:13
  303.5 20.8 %reduce-scatter.5.cloned.1.call-done = f32[40,512]{1,0:T(8,128)} async-done(((f32[40,2048]{1,0:T(8,128)}), f32[40,512]{1,0:T(8,128)}) %reduce-scatter.5.cloned.1.call-update) | async-done | bytes 81936 | tf_op jit(solution)/shard_map/reduce_scatter | solution.py:116
  331.2 9.4 %all_gather.273 = bf16[40,4096]{1,0:T(8,128)(2,1)S(1)} all-gather(bf16[40,512]{1,0:T(8,128)(2,1)S(1)} %collective-permute-done.1), channel_id=1, replica_groups=mesh['pair'=4,'src'=2,'tgt'=4] {'src','tgt'}, dimensions={1}, use_global_device_ids=true | all-gather | bytes 368640 | tf_op jit(solution)/shard_map/all_gather | solution.py:121
  344.5 19.6 %reduce-scatter.7.cloned.1.call-done = f32[40,512]{1,0:T(8,128)} async-done(((f32[40,2048]{1,0:T(8,128)}), f32[40,512]{1,0:T(8,128)}) %reduce-scatter.7.cloned.1.call-update) | async-done | bytes 81936 | tf_op jit(solution)/shard_map/reduce_scatter | solution.py:116
  370.9 9.6 %all_gather.274 = bf16[40,4096]{1,0:T(8,128)(2,1)S(1)} all-gather(bf16[40,512]{1,0:T(8,128)(2,1)S(1)} %collective-permute-done.2), channel_id=1, replica_groups=mesh['pair'=4,'src'=2,'tgt'=4] {'src','tgt'}, dimensions={1}, use_global_device_ids=true | all-gather | bytes 368640 | tf_op jit(solution)/shard_map/all_gather | solution.py:121
  384.4 19.6 %reduce-scatter.9.cloned.1.call-done = f32[40,512]{1,0:T(8,128)} async-done(((f32[40,2048]{1,0:T(8,128)}), f32[40,512]{1,0:T(8,128)}) %reduce-scatter.9.cloned.1.call-update) | async-done | bytes 81936 | tf_op jit(solution)/shard_map/reduce_scatter | solution.py:116
  410.7 9.4 %all_gather.275 = bf16[40,4096]{1,0:T(8,128)(2,1)S(1)} all-gather(bf16[40,512]{1,0:T(8,128)(2,1)S(1)} %collective-permute-done.3), channel_id=1, replica_groups=mesh['pair'=4,'src'=2,'tgt'=4] {'src','tgt'}, dimensions={1}, use_global_device_ids=true | all-gather | bytes 368640 | tf_op jit(solution)/shard_map/all_gather | solution.py:121
  424.5 19.1 %reduce-scatter.11.cloned.1.call-done = f32[40,512]{1,0:T(8,128)} async-done(((f32[40,2048]{1,0:T(8,128)}), f32[40,512]{1,0:T(8,128)}) %reduce-scatter.11.cloned.1.call-update) | async-done | bytes 81936 | tf_op jit(solution)/shard_map/reduce_scatter | solution.py:116
  (238 shorter events, 191.1 us)
Async XLA Ops:
  7.2 317.2 %reduce-scatter.5.cloned.1.call-start = ((), (), s32[]{:S(2)}) async-start(), calls=%async_computation.4 | async-start | bytes 409600 | tf_op jit(solution)/shard_map/reduce_scatter | solution.py:116
  8.2 11.3 %collective-permute-start = (f32[30,2048]{1,0:T(8,128)S(1)}, f32[30,2048]{1,0:T(8,128)S(1)}, u32[]{:S(2)}, u32[]{:S(2)}) collective-permute-start(f32[30,2048]{1,0:T(8,128)S(1)} %bitcast.141), channel_id=1, source_target_pairs={{8,0},{16,8},{24,16},{9,1},{17,9},{25,17},{10,2},{18,10},{26,18},{... | collective-permute-start | bytes 737288 | tf_op jit(solution)/shard_map/ppermute | solution.py:25
  37.6 12.8 %copy-start = (f32[2048,1024]{0,1:T(8,128)}, f32[2048,1024]{0,1:T(8,128)S(1)}, u32[]{:S(2)}) copy-start(f32[2048,1024]{0,1:T(8,128)S(1)} %get-tuple-element.1373) | copy-start | bytes 25165828
  63.4 5.8 %copy-start.1 = (f32[2048,1024]{0,1:T(8,128)S(1)}, f32[2048,1024]{0,1:T(8,128)}, u32[]{:S(2)}) copy-start(f32[2048,1024]{0,1:T(8,128)} %copy-done) | copy-start | bytes 25165828
  94.6 19.1 %slice-start = ((s8[8388608]{0:T(1024)(128)(4,1)}), s8[4194304]{0:T(1024)(128)(4,1)S(1)}, s32[]{:S(2)}) async-start(s8[8388608]{0:T(1024)(128)(4,1)} %bitcast.113), calls=%async_computation.8 | async-start | bytes 8388608
  99.4 14.3 %slice-start.1 = ((s8[8388608]{0:T(1024)(128)(4,1)}), s8[4194304]{0:T(1024)(128)(4,1)S(1)}, s32[]{:S(2)}) async-start(s8[8388608]{0:T(1024)(128)(4,1)} %bitcast.113), calls=%async_computation.9 | async-start | bytes 8388608
  128.0 18.9 %slice-start.2 = ((s8[8388608]{0:T(1024)(128)(4,1)}), s8[4194304]{0:T(1024)(128)(4,1)S(1)}, s32[]{:S(2)}) async-start(s8[8388608]{0:T(1024)(128)(4,1)} %bitcast.115), calls=%async_computation.10 | async-start | bytes 8388608
  132.8 14.1 %slice-start.3 = ((s8[8388608]{0:T(1024)(128)(4,1)}), s8[4194304]{0:T(1024)(128)(4,1)S(1)}, s32[]{:S(2)}) async-start(s8[8388608]{0:T(1024)(128)(4,1)} %bitcast.115), calls=%async_computation.11 | async-start | bytes 8388608
  161.2 19.3 %slice-start.4 = ((s8[8388608]{0:T(1024)(128)(4,1)}), s8[4194304]{0:T(1024)(128)(4,1)S(1)}, s32[]{:S(2)}) async-start(s8[8388608]{0:T(1024)(128)(4,1)} %bitcast.117), calls=%async_computation.12 | async-start | bytes 8388608
  166.0 14.5 %slice-start.5 = ((s8[8388608]{0:T(1024)(128)(4,1)}), s8[4194304]{0:T(1024)(128)(4,1)S(1)}, s32[]{:S(2)}) async-start(s8[8388608]{0:T(1024)(128)(4,1)} %bitcast.117), calls=%async_computation.13 | async-start | bytes 8388608
  194.8 18.9 %slice-start.6 = ((s8[8388608]{0:T(1024)(128)(4,1)}), s8[4194304]{0:T(1024)(128)(4,1)S(1)}, s32[]{:S(2)}) async-start(s8[8388608]{0:T(1024)(128)(4,1)} %bitcast.119), calls=%async_computation.14 | async-start | bytes 8388608
  199.6 14.1 %slice-start.7 = ((s8[8388608]{0:T(1024)(128)(4,1)}), s8[4194304]{0:T(1024)(128)(4,1)S(1)}, s32[]{:S(2)}) async-start(s8[8388608]{0:T(1024)(128)(4,1)} %bitcast.119), calls=%async_computation.15 | async-start | bytes 8388608
  228.0 19.0 %slice-start.8 = ((s8[8388608]{0:T(1024)(128)(4,1)}), s8[4194304]{0:T(1024)(128)(4,1)S(1)}, s32[]{:S(2)}) async-start(s8[8388608]{0:T(1024)(128)(4,1)} %bitcast.121), calls=%async_computation.16 | async-start | bytes 8388608
  232.7 14.3 %slice-start.9 = ((s8[8388608]{0:T(1024)(128)(4,1)}), s8[4194304]{0:T(1024)(128)(4,1)S(1)}, s32[]{:S(2)}) async-start(s8[8388608]{0:T(1024)(128)(4,1)} %bitcast.121), calls=%async_computation.17 | async-start | bytes 8388608
  261.3 18.9 %slice-start.10 = ((s8[8388608]{0:T(1024)(128)(4,1)}), s8[4194304]{0:T(1024)(128)(4,1)S(1)}, s32[]{:S(2)}) async-start(s8[8388608]{0:T(1024)(128)(4,1)} %bitcast.123), calls=%async_computation.18 | async-start | bytes 8388608
  266.1 14.1 %slice-start.11 = ((s8[8388608]{0:T(1024)(128)(4,1)}), s8[4194304]{0:T(1024)(128)(4,1)S(1)}, s32[]{:S(2)}) async-start(s8[8388608]{0:T(1024)(128)(4,1)} %bitcast.123), calls=%async_computation.19 | async-start | bytes 8388608
  283.9 17.3 %copy-start.3 = (f32[40,1024]{1,0:T(8,128)S(1)}, f32[40,1024]{1,0:T(8,128)}, u32[]{:S(2)}) copy-start(f32[40,1024]{1,0:T(8,128)} %param.25) | copy-start | bytes 491524
  299.3 1.9 copy-start.2
  302.8 61.3 %reduce-scatter.7.cloned.1.call-start = ((), (), s32[]{:S(2)}) async-start(), calls=%async_computation.5 | async-start | bytes 409600 | tf_op jit(solution)/shard_map/reduce_scatter | solution.py:116
  325.2 118.3 %copy-start.4 = (f32[40,512]{1,0:T(8,128)S(1)}, f32[40,512]{1,0:T(8,128)}, u32[]{:S(2)}) copy-start(f32[40,512]{1,0:T(8,128)} %reduce-scatter.5.cloned.1.call-done) | copy-start | bytes 245764
  325.2 6.0 %collective-permute-start.1 = (bf16[40,512]{1,0:T(8,128)(2,1)S(1)}, bf16[40,512]{1,0:T(8,128)(2,1)S(1)}, u32[]{:S(2)}, u32[]{:S(2)}) collective-permute-start(bf16[40,512]{1,0:T(8,128)(2,1)S(1)} %select_convert_fusion.2), channel_id=1, source_target_pairs={{8,0},{16,8},{24,16},{9,1},{17,9},{25,17},{10,2},{18,10},{26,18},{... | collective-permute-start | bytes 122888 | tf_op jit(solution)/shard_map/ppermute | solution.py:25
  344.4 59.5 %reduce-scatter.9.cloned.1.call-start = ((), (), s32[]{:S(2)}) async-start(), calls=%async_computation.6 | async-start | bytes 409600 | tf_op jit(solution)/shard_map/reduce_scatter | solution.py:116
  364.1 79.4 %copy-start.5 = (f32[40,512]{1,0:T(8,128)S(1)}, f32[40,512]{1,0:T(8,128)}, u32[]{:S(2)}) copy-start(f32[40,512]{1,0:T(8,128)} %reduce-scatter.7.cloned.1.call-done) | copy-start | bytes 245764
  365.0 5.9 %collective-permute-start.2 = (bf16[40,512]{1,0:T(8,128)(2,1)S(1)}, bf16[40,512]{1,0:T(8,128)(2,1)S(1)}, u32[]{:S(2)}, u32[]{:S(2)}) collective-permute-start(bf16[40,512]{1,0:T(8,128)(2,1)S(1)} %select_convert_fusion.1), channel_id=1, source_target_pairs={{8,0},{16,8},{24,16},{9,1},{17,9},{25,17},{10,2},{18,10},{26,18},{... | collective-permute-start | bytes 122888 | tf_op jit(solution)/shard_map/ppermute | solution.py:25
  384.3 59.2 %reduce-scatter.11.cloned.1.call-start = ((), (), s32[]{:S(2)}) async-start(), calls=%async_computation.7 | async-start | bytes 409600 | tf_op jit(solution)/shard_map/reduce_scatter | solution.py:116
  404.8 5.9 %collective-permute-start.3 = (bf16[40,512]{1,0:T(8,128)(2,1)S(1)}, bf16[40,512]{1,0:T(8,128)(2,1)S(1)}, u32[]{:S(2)}, u32[]{:S(2)}) collective-permute-start(bf16[40,512]{1,0:T(8,128)(2,1)S(1)} %select_convert_fusion), channel_id=1, source_target_pairs={{8,0},{16,8},{24,16},{9,1},{17,9},{25,17},{10,2},{18,10},{26,18},{... | collective-permute-start | bytes 122888 | tf_op jit(solution)/shard_map/ppermute | solution.py:25
Sparse Core Ops, SparseCore 0:
  302.9 21.3 reduce-scatter.4
  344.6 19.4 reduce-scatter.6
  384.4 19.4 reduce-scatter.8
  424.0 19.4 reduce-scatter.10
